TPU v7x, 128 devices: a whole 4x4x4 slice. The times are simulated.
128 devices in a mesh: section: 2 (over x_lo), tok: 8 (over x_hi, z), mdl: 8 (over y, core).
Axes of the slice: x: 4 (x_hi: 2, x_lo: 2; x = x_hi * 2 + x_lo), y: 4, z: 4, core: 2. Of those that a mesh axis runs over, the one named last changes fastest.
Arguments:
- layer_input: bfloat16 [2, 2048, 2048], P(None, 'tok'), may hold values from -6 to 6
- segment_ids: int32 [2, 2048], replicated, may hold values from 0 to 3, as said below
- route_ids: int32 [2, 2048, 6], P(None, ('tok', 'mdl')), may hold values from 0 to 63, all different within a row; in each aligned block of 32 rows (0 to 31, 32 to 63, ..., all dimensions but the last counted through in order) at most 4 rows name the same one
- route_weights: float32 [2, 2048, 6], P(None, ('tok', 'mdl')), may hold values from 0.1 to 0.5
- attn_gain: float32 [2048], replicated, may hold values from 0.5 to 1.5
- w_query: bfloat16 [2048, 3072], P(None, 'mdl'), may hold values from -6.629126 to 6.629126
- w_kv_down: bfloat16 [2048, 576], replicated, may hold values from -0.13258252 to 0.13258252
- latent_gain: float32 [512], replicated, may hold values from 0.5 to 1.5
- w_kv_up: bfloat16 [512, 4096], P(None, 'mdl'), may hold values from -0.25 to 0.25
- w_out: bfloat16 [2048, 2048], P('mdl'), may hold values from -0.125 to 0.125
- ffn_gain: float32 [2048], replicated, may hold values from 0.5 to 1.5
- w_shared_gate: bfloat16 [2048, 2048], P(None, 'mdl'), may hold values from -0.125 to 0.125
- w_shared_up: bfloat16 [2048, 2048], P(None, 'mdl'), may hold values from -0.125 to 0.125
- w_shared_down: bfloat16 [2048, 2048], P('mdl'), may hold values from -0.125 to 0.125
- w_expert_gate: bfloat16 [64, 2048, 768], P(('tok', 'mdl')), may hold values from -0.125 to 0.125
- w_expert_up: bfloat16 [64, 2048, 768], P(('tok', 'mdl')), may hold values from -0.125 to 0.125
- w_expert_down: bfloat16 [64, 768, 2048], P(('tok', 'mdl')), may hold values from -0.21875 to 0.21875
Outputs:
- layer_output: bfloat16 [2, 2048, 2048], P('section', ('tok', 'mdl'))
Inputs may be any that keep to these rules, and one draw needn't show every extreme that they name: `segment_ids`: segment numbers never fall along a pack; each segment has 1 to 1024 tokens and one has exactly 1024. `route_ids`: each token names 6 different experts. In each aligned block of 32 tokens of a pack (the tokens of one device), no expert is named by more than 4 tokens, a bound that some block reaches.
All inputs are finite; a program needn't handle non-finite values.
Results may differ from a plain program's by a relative error of at most 0.02.
Values may be sent and summed in bfloat16 or wider, within the bound.
No kernel may reach another device: no remote copies, remote signals or barrier semaphores. Data moves between devices by JAX's collectives and lax.ppermute only.
A program may use at most 128 MiB of HBM per device.

v0:
```python
import math
import jax
import jax.numpy as jnp
from jax import lax
from jax.sharding import PartitionSpec as P

NOPE = 128
ROPE = 64
VDIM = 128
LATENT = 512
SEGS = 4
EPS = 1e-06


def passed_along(value, axis, steps):
    count = lax.axis_size(axis)
    initial, last = (max(0, -steps), min(count, count - steps))
    return lax.ppermute(value, axis, [(source, source + steps) for source in range(initial, last)])


def rms_scale(values, gain_vec):
    values = values.astype(jnp.float32)
    return values * lax.rsqrt(jnp.mean(values * values, axis=-1, keepdims=True) + EPS) * gain_vec


def rotary(values, positions):
    half_width = values.shape[-1] // 2
    frequency = 10000.0 ** (-jnp.arange(half_width, dtype=jnp.float32) / half_width)
    angles = positions.astype(jnp.float32)[:, None] * frequency[None, :]
    if values.ndim == 3:
        angles = angles[:, None, :]
    cosine = jnp.cos(angles)
    sine_part = jnp.sin(angles)
    lead_half = values[..., :half_width]
    tail_half = values[..., half_width:]
    return jnp.concatenate(
        [lead_half * cosine - tail_half * sine_part, lead_half * sine_part + tail_half * cosine],
        axis=-1,
    )


def positions_of(segment_row, segment_count):
    labels = jnp.arange(segment_count, dtype=jnp.int32)
    starts = jnp.sum((segment_row[None, :] < labels[:, None]).astype(jnp.int32), axis=1)
    member = (segment_row[:, None] == labels[None, :]).astype(jnp.int32)
    return jnp.arange(segment_row.shape[0], dtype=jnp.int32) - jnp.sum(
        member * starts[None, :], axis=1
    )


def shards(
    layer_input,
    segment_ids,
    route_ids,
    route_weights,
    attn_gain,
    w_query,
    w_kv_down,
    latent_gain,
    w_kv_up,
    w_out,
    ffn_gain,
    w_shared_gate,
    w_shared_up,
    w_shared_down,
    w_expert_gate,
    w_expert_up,
    w_expert_down,
):
    n_mdl = lax.axis_size("mdl")
    n_wide = lax.axis_size(("tok", "mdl"))
    section_id = lax.axis_index("section")
    tok_rank = lax.axis_index("tok")
    mdl_rank = lax.axis_index("mdl")
    micro_count, tok_dev, model_width = layer_input.shape
    row_dev = tok_dev // n_mdl
    top_count = route_ids.shape[2]
    local_heads = w_out.shape[0] // VDIM
    qk_width = NOPE + ROPE
    score_scale = 1.0 / math.sqrt(qk_width)
    expert_dev = w_expert_gate.shape[0]
    expert_total = expert_dev * n_wide
    capacity = max(2, 3 * row_dev * top_count // (2 * expert_total))
    slot_total = expert_total * capacity
    slot_ids = jnp.arange(slot_total, dtype=jnp.int32)
    expert_labels = jnp.arange(expert_total, dtype=jnp.int32)
    segment_row = lax.dynamic_index_in_dim(segment_ids, section_id, 0, keepdims=False)
    rows_in = lax.dynamic_index_in_dim(layer_input, section_id, 0, keepdims=False)
    expert_ids = lax.dynamic_index_in_dim(route_ids, section_id, 0, keepdims=False).reshape(-1)
    weight_rows = lax.dynamic_index_in_dim(route_weights, section_id, 0, keepdims=False)
    positions = positions_of(segment_row, SEGS)
    query_start = tok_rank * tok_dev
    query_pos = lax.dynamic_slice_in_dim(positions, query_start, tok_dev)
    query_seg = lax.dynamic_slice_in_dim(segment_row, query_start, tok_dev)
    query_index = query_start + jnp.arange(tok_dev, dtype=jnp.int32)
    normed = rms_scale(rows_in, attn_gain).astype(jnp.bfloat16)
    queries = jnp.dot(normed, w_query, preferred_element_type=jnp.float32).reshape(
        tok_dev, local_heads, qk_width
    )
    queries = jnp.concatenate(
        [queries[..., :NOPE], rotary(queries[..., NOPE:], query_pos)], axis=-1
    ).astype(jnp.bfloat16)
    compressed = jnp.dot(normed, w_kv_down, preferred_element_type=jnp.float32)
    latent = rms_scale(compressed[:, :LATENT], latent_gain).astype(jnp.bfloat16)
    key_rope = rotary(compressed[:, LATENT:], query_pos).astype(jnp.bfloat16)
    kv_rows = lax.all_gather(
        jnp.concatenate([latent, key_rope], axis=-1), "tok", axis=0, tiled=True
    )
    key_count = kv_rows.shape[0]
    expanded = (
        jnp.dot(kv_rows[:, :LATENT], w_kv_up, preferred_element_type=jnp.float32)
        .astype(jnp.bfloat16)
        .reshape(key_count, local_heads, NOPE + VDIM)
    )
    rope_keys = kv_rows[:, LATENT:]
    scores = jnp.einsum(
        "qhd,khd->hqk",
        queries[..., :NOPE],
        expanded[..., :NOPE],
        preferred_element_type=jnp.float32,
    )
    scores = scores + jnp.einsum(
        "qhd,kd->hqk", queries[..., NOPE:], rope_keys, preferred_element_type=jnp.float32
    )
    scores = scores * score_scale
    key_index = jnp.arange(key_count, dtype=jnp.int32)
    allowed = (segment_row[None, :] == query_seg[:, None]) & (
        key_index[None, :] <= query_index[:, None]
    )
    allowed = allowed[None, :, :]
    masked = jnp.where(allowed, scores, -1e30)
    row_max = jnp.max(masked, axis=-1, keepdims=True)
    weights = jnp.where(allowed, jnp.exp(scores - row_max), 0.0)
    totals = jnp.sum(weights, axis=-1, keepdims=True)
    weighted = jnp.einsum(
        "hqk,khd->hqd",
        weights.astype(jnp.bfloat16),
        expanded[..., NOPE:],
        preferred_element_type=jnp.float32,
    )
    attended = (
        (weighted / totals)
        .astype(jnp.bfloat16)
        .transpose(1, 0, 2)
        .reshape(tok_dev, local_heads * VDIM)
    )
    mixed_heads = lax.psum(
        jnp.dot(attended, w_out, preferred_element_type=jnp.float32).astype(jnp.bfloat16), "mdl"
    ).astype(jnp.float32)
    residual = (rows_in.astype(jnp.float32) + mixed_heads).astype(jnp.bfloat16)
    normed_ffn_all = rms_scale(residual, ffn_gain).astype(jnp.bfloat16)
    own_residual = lax.dynamic_slice_in_dim(residual, mdl_rank * row_dev, row_dev)
    normed_ffn = lax.dynamic_slice_in_dim(normed_ffn_all, mdl_rank * row_dev, row_dev)
    gate_proj = jnp.dot(normed_ffn_all, w_shared_gate, preferred_element_type=jnp.float32)
    up_proj = jnp.dot(normed_ffn_all, w_shared_up, preferred_element_type=jnp.float32)
    shared_act = (jax.nn.silu(gate_proj) * up_proj).astype(jnp.bfloat16)
    shared_out = lax.psum_scatter(
        jnp.dot(shared_act, w_shared_down, preferred_element_type=jnp.float32).astype(jnp.bfloat16),
        "mdl",
        scatter_dimension=0,
        tiled=True,
    ).astype(jnp.float32)
    onehot = (expert_ids[:, None] == expert_labels[None, :]).astype(jnp.int32)
    earlier = jnp.cumsum(onehot, axis=0) - onehot
    slot_index = jnp.sum(earlier * onehot, axis=1)
    target = expert_ids * capacity + slot_index
    placing = (
        (slot_ids[:, None] == target[None, :])
        .astype(jnp.int32)
        .reshape(slot_total, row_dev, top_count)
    )
    placing = jnp.sum(placing, axis=2).astype(jnp.bfloat16)
    outgoing = (
        jnp.dot(placing, normed_ffn, preferred_element_type=jnp.float32)
        .astype(jnp.bfloat16)
        .reshape(expert_total, capacity, model_width)
    )
    buffer = lax.all_to_all(outgoing, ("tok", "mdl"), split_axis=0, concat_axis=0, tiled=True)
    item_count = buffer.shape[1]
    grouped = (
        buffer.reshape(n_wide, expert_dev, item_count, model_width)
        .transpose(1, 0, 2, 3)
        .reshape(expert_dev, n_wide * item_count, model_width)
    )
    e_gate = jnp.einsum("erd,edf->erf", grouped, w_expert_gate, preferred_element_type=jnp.float32)
    e_up = jnp.einsum("erd,edf->erf", grouped, w_expert_up, preferred_element_type=jnp.float32)
    expert_act = (jax.nn.silu(e_gate) * e_up).astype(jnp.bfloat16)
    produced = jnp.einsum(
        "erf,efd->erd", expert_act, w_expert_down, preferred_element_type=jnp.float32
    ).astype(jnp.bfloat16)
    processed = (
        produced.reshape(expert_dev, n_wide, item_count, model_width)
        .transpose(1, 0, 2, 3)
        .reshape(n_wide * expert_dev, item_count, model_width)
    )
    returned = lax.all_to_all(processed, ("tok", "mdl"), split_axis=0, concat_axis=0, tiled=True)
    matched = target.reshape(row_dev, top_count)[:, :, None] == slot_ids[None, None, :]
    combining = jnp.sum(jnp.where(matched, weight_rows[:, :, None], 0.0), axis=1)
    routed = jnp.dot(
        combining,
        returned.reshape(slot_total, model_width).astype(jnp.float32),
        precision=lax.Precision.HIGHEST,
    )
    finished = (own_residual.astype(jnp.float32) + shared_out + routed).astype(jnp.bfloat16)
    return finished[None]


def solution(mesh):
    in_specs = (
        P(None, "tok", None),
        P(),
        P(None, ("tok", "mdl"), None),
        P(None, ("tok", "mdl"), None),
        P(),
        P(None, "mdl"),
        P(),
        P(),
        P(None, "mdl"),
        P("mdl", None),
        P(),
        P(None, "mdl"),
        P(None, "mdl"),
        P("mdl", None),
        P(("tok", "mdl"), None, None),
        P(("tok", "mdl"), None, None),
        P(("tok", "mdl"), None, None),
    )
    out_specs = P("section", ("tok", "mdl"), None)
    return jax.shard_map(shards, mesh=mesh, in_specs=in_specs, out_specs=out_specs, check_vma=False)
```

profile of v0, /device:TPU:1, one launch (start us, length us, event | category | flops | bytes accessed | tf_op | source)
XLA Modules:
  0.0 237.3 jit_solution(6687160402400603476)
XLA Ops:
  6.6 0.9 constant_dynamic-slice_fusion.2
  7.7 1.5 fusion.22
  9.2 2.9 %fusion.53 = f32[256,576]{0,1:T(8,128)S(1)} fusion(bf16[2048,576]{0,1:T(8,128)(2,1)} %param.23, f32[2048]{0:T(1024)} %param.21, f32[256]{0:T(256)S(1)} %add_rsqrt_fusion.2, bf16[2,256,2048]{2,1,0:T(8,128)(2,1)} %param.17, s32[]{:T(128)S(6)} %select_n.33), kind=kOutput, calls=%fused_computation.52 | convolution fusion | flops 606076928 | bytes 4006916 | tf_op jit(solution)/shard_map/dot_general | solution.py:103
  13.1 1.0 multiply_cosine_fusion
  14.1 1.2 multiply_convert_fusion
  16.1 2.6 %copy.37 = bf16[2048,384]{0,1:T(8,128)(2,1)} copy(bf16[2048,384]{1,0:T(8,128)(2,1)} %param.22) | data formatting | bytes 3145728 | tf_op args[5]
  20.6 2.4 %fusion.51 = f32[256,2,192]{0,2,1:T(8,128)S(1)} fusion(bf16[2,192,2048]{2,1,0:T(8,128)(2,1)} %bitcast.95, f32[2048]{0:T(1024)S(1)} %copy-done.14, f32[256]{0:T(256)S(1)} %add_rsqrt_fusion.2, bf16[2,256,2048]{2,1,0:T(8,128)(2,1)} %param.17, s32[]{:T(128)S(6)} %select_n.33), kind=kOutput, calls=%fused_computation.51 | convolution fusion | flops 404750336 | bytes 3023876 | tf_op jit(solution)/shard_map/dot_general | solution.py:97
  23.8 1.5 fusion.32
  25.3 49.9 %all-gather.2.cloned.1.call-done = bf16[2048,576]{0,1:T(8,128)(2,1)} async-done(((bf16[256,576]{0,1:T(8,128)(2,1)}), bf16[2048,576]{0,1:T(8,128)(2,1)}) %all-gather.2.cloned.1.call-update) | async-done | bytes 2359312 | tf_op jit(solution)/shard_map/all_gather | solution.py:106
  75.3 3.0 %convolution_convert_fusion = bf16[2048,512]{0,1:T(8,128)(2,1)S(1)} fusion(bf16[512,512]{1,0:T(8,128)(2,1)} %param.25, bf16[2048,576]{0,1:T(8,128)(2,1)} %all-gather.2.cloned.1.call-done), kind=kOutput, calls=%fused_computation.12 | convolution fusion | flops 1074790400 | bytes 4718592 | tf_op jit(solution)/shard_map/dot_general | solution.py:111
  79.6 1.8 fusion.1
  81.4 1.7 fusion.99
  83.3 5.4 %fusion.47 = bf16[256,2,128]{0,2,1:T(8,128)(2,1)S(1)} fusion(bf16[2048,2,256]{0,2,1:T(8,128)(2,1)} %bitcast.97, f32[256,2]{0,1:T(2,128)S(1)} %bitcast.104, f32[2,256,2048]{2,1,0:T(8,128)} %copy-done.3, pred[256,2048]{1,0:T(8,128)(4,1)} %fusion.32), kind=kOutput, calls=%fused_computation.49 | convolution fusion | flops 272763392 | bytes 10618880 | tf_op jit(solution)/shard_map/hqk,khd->hqd/dot_general | solution.py:135
  88.8 2.7 %convolution_convert_fusion.2 = bf16[256,2048]{1,0:T(8,128)(2,1)} fusion(bf16[256,256]{0,1:T(8,128)(2,1)S(1)} %bitcast.101, bf16[256,2048]{1,0:T(8,128)(2,1)} %param.26), kind=kOutput, calls=%fused_computation.21 | convolution fusion | flops 268959744 | bytes 2228224 | tf_op jit(solution)/shard_map/dot_general | solution.py:148
  92.0 59.0 %all-reduce.3.cloned.1.call-done = bf16[256,2048]{1,0:T(8,128)(2,1)} async-done(((bf16[256,2048]{1,0:T(8,128)(2,1)}), bf16[256,2048]{1,0:T(8,128)(2,1)}) %all-reduce.3.cloned.1.call-update) | async-done | bytes 1048592 | tf_op jit(solution)/shard_map/psum | solution.py:147
  150.9 2.0 fusion.19
  153.0 1.0 copy-done.2
  154.3 1.0 copy-done.1
  155.3 1.5 convolution_convert_fusion.3
  156.7 2.3 reshape.251
  159.0 10.7 %all-to-all-start = ((bf16[64,4,2048]{2,1,0:T(4,128)(2,1)}), bf16[64,4,2048]{2,1,0:T(4,128)(2,1)}, u32[]{:S(2)}, u32[]{:S(2)}) async-start(bf16[64,4,2048]{2,1,0:T(4,128)(2,1)} %reshape.251), calls=%async_computation.1 | async-start | bytes 2097152 | tf_op jit(solution)/shard_map/all_to_all | solution.py:178
  169.8 2.0 fusion.100
  171.8 4.2 %convolution_convert_fusion.1 = bf16[256,2048]{1,0:T(8,128)(2,1)} fusion(bf16[256,2048]{1,0:T(8,128)(2,1)} %param.30, bf16[256,2048]{1,0:T(8,128)(2,1)} %copy-done.1, bf16[2048,256]{1,0:T(8,128)(2,1)} %param.29, f32[256,256]{1,0:T(8,128)S(1)} %fusion.100), kind=kOutput, calls=%fused_computation.20 | convolution fusion | flops 537788416 | bytes 4456448 | tf_op jit(solution)/shard_map/dot_general | solution.py:158
  176.0 12.2 %all-to-all-done = bf16[64,4,2048]{2,1,0:T(4,128)(2,1)} async-done(((bf16[64,4,2048]{2,1,0:T(4,128)(2,1)}), bf16[64,4,2048]{2,1,0:T(4,128)(2,1)}, u32[]{:S(2)}, u32[]{:S(2)}) %all-to-all-start) | async-done | bytes 1048608 | tf_op jit(solution)/shard_map/all_to_all | solution.py:178
  188.2 2.1 reshape.252
  190.3 4.1 %fusion.9 = f32[256,768]{1,0:T(8,128)} fusion(bf16[256,2048]{1,0:T(8,128)(2,1)} %reshape.252, bf16[1,2048,768]{2,1,0:T(8,128)(2,1)} %param.31), kind=kOutput, calls=%fused_computation.10 | convolution fusion | flops 805306368 | bytes 4980736 | tf_op jit(solution)/shard_map/erd,edf->erf/dot_general | solution.py:185
  194.4 5.5 %fusion.14 = bf16[256,2048]{1,0:T(8,128)(2,1)} fusion(bf16[1,768,2048]{2,1,0:T(8,128)(2,1)S(1)} %copy-done, bf16[256,2048]{1,0:T(8,128)(2,1)} %reshape.252, bf16[1,2048,768]{2,1,0:T(8,128)(2,1)} %param.32, f32[256,768]{1,0:T(8,128)} %fusion.9), kind=kOutput, calls=%fused_computation.22 | convolution fusion | flops 1612316672 | bytes 9175040 | tf_op jit(solution)/shard_map/erf,efd->erd/dot_general | solution.py:188
  200.0 2.3 reshape_transpose_reshape.4
  202.3 5.4 %all-to-all-start.1 = ((bf16[64,4,2048]{2,1,0:T(4,128)(2,1)}), bf16[64,4,2048]{2,1,0:T(4,128)(2,1)}, u32[]{:S(2)}, u32[]{:S(2)}) async-start(bf16[64,4,2048]{2,1,0:T(4,128)(2,1)} %reshape_transpose_reshape.4), calls=%async_computation.2 | async-start | bytes 2097152 | tf_op jit(solution)/shard_map/all_to_all | solution.py:196
  207.8 18.3 %all-to-all-done.1 = bf16[64,4,2048]{2,1,0:T(4,128)(2,1)} async-done(((bf16[64,4,2048]{2,1,0:T(4,128)(2,1)}), bf16[64,4,2048]{2,1,0:T(4,128)(2,1)}, u32[]{:S(2)}, u32[]{:S(2)}) %all-to-all-start.1) | async-done | bytes 1048608 | tf_op jit(solution)/shard_map/all_to_all | solution.py:196
  226.1 2.1 reshape.256
  228.2 2.6 %fusion.18 = bf16[1,32,2048]{2,1,0:T(8,128)(2,1)} fusion(f32[32,256]{1,0:T(8,128)S(1)} %select_reduce_fusion.1, bf16[256,2048]{1,0:T(8,128)(2,1)} %reshape.256, bf16[32,2048]{1,0:T(8,128)(2,1)} %reduce-scatter.2.cloned.1.call-done, bf16[256,2048]{1,0:T(8,128)(2,1)} %copy-done.2, s32[]{:T(128)S(6)} %select_n.39), kind=kOutput, calls=%fused_computation.26 | convolution fusion | flops 201654272 | bytes 1474564 | tf_op jit(solution)/shard_map/dot_general | solution.py:199
  (68 shorter events, 7.0 us)
Async XLA Ops:
  6.5 187.9 %copy-start = (bf16[1,768,2048]{2,1,0:T(8,128)(2,1)S(1)}, bf16[1,768,2048]{2,1,0:T(8,128)(2,1)}, u32[]{:S(2)}) copy-start(bf16[1,768,2048]{2,1,0:T(8,128)(2,1)} %param.33) | copy-start | bytes 9437188
  6.5 68.7 %all-gather.2.cloned.1.call-start = ((), (), s32[]{:S(2)}) async-start(), calls=%async_computation.3 | async-start | bytes 2654208 | tf_op jit(solution)/shard_map/all_gather | solution.py:106
  9.2 4.9 %copy-start.11 = (f32[512]{0:T(512)S(1)}, f32[512]{0:T(512)}, u32[]{:S(2)}) copy-start(f32[512]{0:T(512)} %param.24) | copy-start | bytes 6148
  12.1 0.8 copy-start.4
  14.1 4.7 %copy-start.12 = (s32[2,32,6]{1,0,2:T(2,128)S(1)}, s32[2,32,6]{1,0,2:T(2,128)}, u32[]{:S(2)}) copy-start(s32[2,32,6]{1,0,2:T(2,128)} %param.19) | copy-start | bytes 4612
  15.3 5.3 %copy-start.14 = (f32[2048]{0:T(1024)S(1)}, f32[2048]{0:T(1024)}, u32[]{:S(2)}) copy-start(f32[2048]{0:T(1024)} %param.21) | copy-start | bytes 24580
  16.1 134.9 %all-reduce.3.cloned.1.call-start = ((), (), s32[]{:S(2)}) async-start(), calls=%async_computation.4 | async-start | bytes 2097152 | tf_op jit(solution)/shard_map/psum | solution.py:147
  19.8 5.5 %copy-start.10 = (s32[64,3]{0,1:T(4,128)}, s32[64,3]{0,1:T(4,128)S(1)}, u32[]{:S(2)}) copy-start(s32[64,3]{0,1:T(4,128)S(1)} %reduce-window.9) | copy-start | bytes 2308
  23.0 0.7 copy-start.7
  75.3 3.0 %copy-start.8 = (f32[256,2,192]{0,2,1:T(8,128)S(1)}, f32[256,2,192]{0,2,1:T(8,128)}, u32[]{:S(2)}) copy-start(f32[256,2,192]{0,2,1:T(8,128)} %copy-done.7) | copy-start | bytes 1179652
  78.3 1.3 copy-start.6
  79.6 1.8 copy-start.5
  81.4 1.9 copy-start.3
  88.8 2.8 %slice-start = ((s32[64,3]{0,1:T(4,128)}), s32[64,2]{0,1:T(2,128)S(1)}, s32[]{:S(2)}) async-start(s32[64,3]{0,1:T(4,128)} %copy-done.10), calls=%async_computation.6 | async-start | bytes 2048 | tf_op jit(solution)/shard_map/slice.1
  91.5 62.5 %copy-start.9 = (f32[2048]{0:T(1024)S(1)}, f32[2048]{0:T(1024)}, u32[]{:S(2)}) copy-start(f32[2048]{0:T(1024)} %param.27) | copy-start | bytes 24580
  153.0 1.0 copy-start.2
  154.3 1.0 copy-start.1
  159.0 29.2 %all-to-all-start = ((bf16[64,4,2048]{2,1,0:T(4,128)(2,1)}), bf16[64,4,2048]{2,1,0:T(4,128)(2,1)}, u32[]{:S(2)}, u32[]{:S(2)}) async-start(bf16[64,4,2048]{2,1,0:T(4,128)(2,1)} %reshape.251), calls=%async_computation.1 | async-start | bytes 2097152 | tf_op jit(solution)/shard_map/all_to_all | solution.py:178
  169.7 58.5 %reduce-scatter.2.cloned.1.call-start = ((), (), s32[]{:S(2)}) async-start(), calls=%async_computation.5 | async-start | bytes 1179648 | tf_op jit(solution)/shard_map/reduce_scatter | solution.py:157
  200.0 7.7 %copy-start.13 = (f32[2,32,6]{1,0,2:T(2,128)S(1)}, f32[2,32,6]{1,0,2:T(2,128)}, u32[]{:S(2)}) copy-start(f32[2,32,6]{1,0,2:T(2,128)} %param.20) | copy-start | bytes 4612
  202.3 23.8 %all-to-all-start.1 = ((bf16[64,4,2048]{2,1,0:T(4,128)(2,1)}), bf16[64,4,2048]{2,1,0:T(4,128)(2,1)}, u32[]{:S(2)}, u32[]{:S(2)}) async-start(bf16[64,4,2048]{2,1,0:T(4,128)(2,1)} %reshape_transpose_reshape.4), calls=%async_computation.2 | async-start | bytes 2097152 | tf_op jit(solution)/shard_map/all_to_all | solution.py:196
Sparse Core Ops, SparseCore 0:
  16.2 59.0 all-gather.1
  91.6 59.2 all-reduce.2
  176.1 30.7 reduce-scatter.1
where the time goes:
time: 238 us; the launch traced here: 237 us
  waiting for transfers between devices  139 us (58%)
  matrix products  38.8 us (16%)
  local copies, waits for them, and re-layouts  18 us (8%)
  starting transfers between devices  16.2 us (7%)
  between operations  13.4 us (6%)
  other arithmetic  11.5 us (5%)
    psum x1, waiting for transfers between devices, shards(): lax.psum(jnp.dot(attended, w_out, preferred_element_type=jnp.float32).ast...  59 us
    all_gather x1, waiting for transfers between devices, shards(): lax.all_gather(jnp.concatenate([latent, key_rope], axis=-1), 'tok', axis=...  49.9 us
    all_to_all x1, waiting for transfers between devices, shards(): lax.all_to_all(processed, ('tok', 'mdl'), split_axis=0, concat_axis=0, ti...  18.3 us
    all_to_all x1, waiting for transfers between devices, shards(): lax.all_to_all(outgoing, ('tok', 'mdl'), split_axis=0, concat_axis=0, til...  12.2 us
    all_to_all x1, starting transfers between devices, shards(): lax.all_to_all(outgoing, ('tok', 'mdl'), split_axis=0, concat_axis=0, til...  10.7 us
    unnamed x32, local copies, waits for them, and re-layouts  6.91 us
    dot_general x1, matrix products, shards(): jnp.einsum('erf,efd->erd', expert_act, w_expert_down, preferred_element_t...  5.54 us
    dot_general x1, matrix products, shards(): jnp.einsum('hqk,khd->hqd', weights.astype(jnp.bfloat16), expanded[..., NO...  5.43 us
  transfers between devices with their start and end apart: 5, of which 4 were waited for; matrix products, arithmetic and copies ran while one was open for 13% of the time, Pallas kernels for 0%

commit v1 on v0

--- a/solution.py
+++ b/solution.py
@@ -103,8 +103,14 @@
     compressed = jnp.dot(normed, w_kv_down, preferred_element_type=jnp.float32)
     latent = rms_scale(compressed[:, :LATENT], latent_gain).astype(jnp.bfloat16)
     key_rope = rotary(compressed[:, LATENT:], query_pos).astype(jnp.bfloat16)
-    kv_rows = lax.all_gather(
-        jnp.concatenate([latent, key_rope], axis=-1), "tok", axis=0, tiled=True
+    kv_rows = jnp.concatenate(
+        lax.all_to_all(
+            jnp.stack([jnp.concatenate([latent, key_rope], axis=-1)] * lax.axis_size("tok")),
+            "tok",
+            0,
+            0,
+        ),
+        axis=0,
     )
     key_count = kv_rows.shape[0]
     expanded = (

time: 238 us -> 219 us (0.920)
  waiting for transfers between devices: 139 us -> 111 us
  starting transfers between devices: 16.2 us -> 24.7 us
  local copies, waits for them, and re-layouts: 18 us -> 21.8 us
  matrix products: 38.8 us -> 36.1 us
    all_gather x1 -> x0, waiting for transfers between devices: 49.9 us -> none  [shards(): lax.all_gather(jnp.concatenate([latent, key_rope], axis=-1), 'tok', axis=...]
    all_to_all x0 -> x1, waiting for transfers between devices: none -> 19.8 us  [shards(): lax.all_to_all(jnp.stack([jnp.concatenate([latent, key_rope], axis=-1)] *...]
    all_to_all x0 -> x1, starting transfers between devices: none -> 8.31 us  [shards(): lax.all_to_all(jnp.stack([jnp.concatenate([latent, key_rope], axis=-1)] *...]
    unnamed x32 -> x34, local copies, waits for them, and re-layouts: 6.91 us -> 7.19 us
  transfers between devices with their start and end apart: 5 -> 5, of which waited for: 4 -> 4; matrix products, arithmetic and copies ran while one was open for 13% -> 14% of each run, Pallas kernels for 0% -> 0%
where the time goes in v1:
time: 219 us; the launch traced here: 218 us
  waiting for transfers between devices  111 us (51%)
  matrix products  36.1 us (16%)
  starting transfers between devices  24.7 us (11%)
  local copies, waits for them, and re-layouts  21.8 us (10%)
  between operations  13.7 us (6%)
  other arithmetic  10.8 us (5%)
    psum x1, waiting for transfers between devices, shards(): lax.psum(jnp.dot(attended, w_out, preferred_element_type=jnp.float32).ast...  60.2 us
    all_to_all x1, waiting for transfers between devices, shards(): lax.all_to_all(jnp.stack([jnp.concatenate([latent, key_rope], axis=-1)] *...  19.8 us
    all_to_all x1, waiting for transfers between devices, shards(): lax.all_to_all(processed, ('tok', 'mdl'), split_axis=0, concat_axis=0, ti...  18.3 us
    all_to_all x1, waiting for transfers between devices, shards(): lax.all_to_all(outgoing, ('tok', 'mdl'), split_axis=0, concat_axis=0, til...  12.2 us
    all_to_all x1, starting transfers between devices, shards(): lax.all_to_all(outgoing, ('tok', 'mdl'), split_axis=0, concat_axis=0, til...  10.9 us
    all_to_all x1, starting transfers between devices, shards(): lax.all_to_all(jnp.stack([jnp.concatenate([latent, key_rope], axis=-1)] *...  8.31 us
    unnamed x34, local copies, waits for them, and re-layouts  7.19 us
    dot_general x1, matrix products, shards(): jnp.einsum('erf,efd->erd', expert_act, w_expert_down, preferred_element_t...  5.53 us
  transfers between devices with their start and end apart: 5, of which 4 were waited for; matrix products, arithmetic and copies ran while one was open for 14% of the time, Pallas kernels for 0%

profile of v1, /device:TPU:1, one launch (start us, length us, event | category | flops | bytes accessed | tf_op | source)
XLA Modules:
  0.0 217.7 jit_solution(15773290859829670427)
XLA Ops:
  7.7 1.5 fusion.22
  9.2 2.9 %fusion.53 = f32[256,576]{0,1:T(8,128)S(1)} fusion(bf16[2048,576]{0,1:T(8,128)(2,1)} %param.23, f32[2048]{0:T(1024)} %param.21, f32[256]{0:T(256)S(1)} %add_rsqrt_fusion.2, bf16[2,256,2048]{2,1,0:T(8,128)(2,1)} %param.17, s32[]{:T(128)S(6)} %select_n.33), kind=kOutput, calls=%fused_computation.52 | convolution fusion | flops 606076928 | bytes 4006916 | tf_op jit(solution)/shard_map/dot_general | solution.py:103
  13.1 1.0 multiply_cosine_fusion
  14.1 1.2 multiply_convert_fusion
  15.3 1.5 stack.2
  16.8 8.3 %all-to-all-start = ((bf16[8,256,576]{1,2,0:T(8,128)(2,1)}), bf16[8,256,576]{1,2,0:T(8,128)(2,1)}, u32[]{:S(2)}, u32[]{:S(2)}) async-start(bf16[8,256,576]{1,2,0:T(8,128)(2,1)} %stack.2), calls=%async_computation | async-start | bytes 4718592 | tf_op jit(solution)/shard_map/all_to_all | solution.py:107
  25.2 2.6 %copy.51 = bf16[2048,384]{0,1:T(8,128)(2,1)} copy(bf16[2048,384]{1,0:T(8,128)(2,1)} %param.22) | data formatting | bytes 3145728 | tf_op args[5]
  29.7 2.4 %fusion.51 = f32[256,2,192]{0,2,1:T(8,128)S(1)} fusion(bf16[2,192,2048]{2,1,0:T(8,128)(2,1)} %bitcast.99, f32[2048]{0:T(1024)S(1)} %copy-done.15, f32[256]{0:T(256)S(1)} %add_rsqrt_fusion.2, bf16[2,256,2048]{2,1,0:T(8,128)(2,1)} %param.17, s32[]{:T(128)S(6)} %select_n.33), kind=kOutput, calls=%fused_computation.51 | convolution fusion | flops 404750336 | bytes 3023876 | tf_op jit(solution)/shard_map/dot_general | solution.py:97
  32.9 1.5 fusion.32
  34.4 19.8 %all-to-all-done = bf16[8,256,576]{1,2,0:T(8,128)(2,1)} async-done(((bf16[8,256,576]{1,2,0:T(8,128)(2,1)}), bf16[8,256,576]{1,2,0:T(8,128)(2,1)}, u32[]{:S(2)}, u32[]{:S(2)}) %all-to-all-start) | async-done | bytes 2359328 | tf_op jit(solution)/shard_map/all_to_all | solution.py:107
  54.3 2.0 copy.69
  56.3 1.3 convolution_convert_fusion
  60.0 1.7 fusion.99
  62.0 5.4 %fusion.47 = bf16[256,2,128]{0,2,1:T(8,128)(2,1)S(1)} fusion(bf16[2048,2,256]{0,2,1:T(8,128)(2,1)} %bitcast.101, f32[256,2]{0,1:T(2,128)S(1)} %bitcast.108, f32[2,256,2048]{2,1,0:T(8,128)} %copy-done.3, pred[256,2048]{1,0:T(8,128)(4,1)} %fusion.32), kind=kOutput, calls=%fused_computation.49 | convolution fusion | flops 272763392 | bytes 10618880 | tf_op jit(solution)/shard_map/hqk,khd->hqd/dot_general | solution.py:141
  67.4 2.7 %convolution_convert_fusion.2 = bf16[256,2048]{1,0:T(8,128)(2,1)} fusion(bf16[256,256]{0,1:T(8,128)(2,1)S(1)} %bitcast.105, bf16[256,2048]{1,0:T(8,128)(2,1)} %param.26), kind=kOutput, calls=%fused_computation.21 | convolution fusion | flops 268959744 | bytes 2228224 | tf_op jit(solution)/shard_map/dot_general | solution.py:154
  70.6 60.2 %all-reduce.3.cloned.1.call-done = bf16[256,2048]{1,0:T(8,128)(2,1)} async-done(((bf16[256,2048]{1,0:T(8,128)(2,1)}), bf16[256,2048]{1,0:T(8,128)(2,1)}) %all-reduce.3.cloned.1.call-update) | async-done | bytes 1048592 | tf_op jit(solution)/shard_map/psum | solution.py:153
  130.8 2.0 fusion.19
  132.9 1.0 copy-done.2
  135.2 1.5 convolution_convert_fusion.3
  136.7 2.3 %reshape.257 = bf16[64,4,2048]{2,1,0:T(4,128)(2,1)} reshape(bf16[256,2048]{1,0:T(8,128)(2,1)} %convolution_convert_fusion.3) | data formatting | bytes 2097152 | tf_op jit(solution)/shard_map/reshape | solution.py:182
  138.9 10.9 %all-to-all-start.1 = ((bf16[64,4,2048]{2,1,0:T(4,128)(2,1)}), bf16[64,4,2048]{2,1,0:T(4,128)(2,1)}, u32[]{:S(2)}, u32[]{:S(2)}) async-start(bf16[64,4,2048]{2,1,0:T(4,128)(2,1)} %reshape.257), calls=%async_computation.2 | async-start | bytes 2097152 | tf_op jit(solution)/shard_map/all_to_all | solution.py:184
  149.9 2.0 fusion.100
  151.9 4.2 %convolution_convert_fusion.1 = bf16[256,2048]{1,0:T(8,128)(2,1)} fusion(bf16[256,2048]{1,0:T(8,128)(2,1)} %param.30, bf16[256,2048]{1,0:T(8,128)(2,1)} %copy-done.1, bf16[2048,256]{1,0:T(8,128)(2,1)} %param.29, f32[256,256]{1,0:T(8,128)S(1)} %fusion.100), kind=kOutput, calls=%fused_computation.20 | convolution fusion | flops 537788416 | bytes 4456448 | tf_op jit(solution)/shard_map/dot_general | solution.py:164
  156.1 12.2 %all-to-all-done.1 = bf16[64,4,2048]{2,1,0:T(4,128)(2,1)} async-done(((bf16[64,4,2048]{2,1,0:T(4,128)(2,1)}), bf16[64,4,2048]{2,1,0:T(4,128)(2,1)}, u32[]{:S(2)}, u32[]{:S(2)}) %all-to-all-start.1) | async-done | bytes 1048608 | tf_op jit(solution)/shard_map/all_to_all | solution.py:184
  168.3 2.1 reshape.258
  170.4 4.1 %fusion.9 = f32[256,768]{1,0:T(8,128)} fusion(bf16[256,2048]{1,0:T(8,128)(2,1)} %reshape.258, bf16[1,2048,768]{2,1,0:T(8,128)(2,1)} %param.31), kind=kOutput, calls=%fused_computation.10 | convolution fusion | flops 805306368 | bytes 4980736 | tf_op jit(solution)/shard_map/erd,edf->erf/dot_general | solution.py:191
  174.5 5.5 %fusion.14 = bf16[256,2048]{1,0:T(8,128)(2,1)} fusion(bf16[1,768,2048]{2,1,0:T(8,128)(2,1)S(1)} %copy-done, bf16[256,2048]{1,0:T(8,128)(2,1)} %reshape.258, bf16[1,2048,768]{2,1,0:T(8,128)(2,1)} %param.32, f32[256,768]{1,0:T(8,128)} %fusion.9), kind=kOutput, calls=%fused_computation.22 | convolution fusion | flops 1612316672 | bytes 9175040 | tf_op jit(solution)/shard_map/erf,efd->erd/dot_general | solution.py:194
  180.1 2.3 %reshape_transpose_reshape.4 = bf16[64,4,2048]{2,1,0:T(4,128)(2,1)} reshape(bf16[256,2048]{1,0:T(8,128)(2,1)} %fusion.14) | data formatting | bytes 2097152 | tf_op jit(solution)/shard_map/reshape;transpose;reshape | solution.py:200
  182.4 5.4 %all-to-all-start.2 = ((bf16[64,4,2048]{2,1,0:T(4,128)(2,1)}), bf16[64,4,2048]{2,1,0:T(4,128)(2,1)}, u32[]{:S(2)}, u32[]{:S(2)}) async-start(bf16[64,4,2048]{2,1,0:T(4,128)(2,1)} %reshape_transpose_reshape.4), calls=%async_computation.3 | async-start | bytes 2097152 | tf_op jit(solution)/shard_map/all_to_all | solution.py:202
  187.9 18.3 %all-to-all-done.2 = bf16[64,4,2048]{2,1,0:T(4,128)(2,1)} async-done(((bf16[64,4,2048]{2,1,0:T(4,128)(2,1)}), bf16[64,4,2048]{2,1,0:T(4,128)(2,1)}, u32[]{:S(2)}, u32[]{:S(2)}) %all-to-all-start.2) | async-done | bytes 1048608 | tf_op jit(solution)/shard_map/all_to_all | solution.py:202
  206.2 2.1 reshape.262
  208.3 2.6 %fusion.18 = bf16[1,32,2048]{2,1,0:T(8,128)(2,1)} fusion(f32[32,256]{1,0:T(8,128)S(1)} %select_reduce_fusion.1, bf16[256,2048]{1,0:T(8,128)(2,1)} %reshape.262, bf16[32,2048]{1,0:T(8,128)(2,1)} %reduce-scatter.2.cloned.1.call-done, bf16[256,2048]{1,0:T(8,128)(2,1)} %copy-done.2, s32[]{:T(128)S(6)} %select_n.39), kind=kOutput, calls=%fused_computation.26 | convolution fusion | flops 201654272 | bytes 1474564 | tf_op jit(solution)/shard_map/dot_general | solution.py:205
  (71 shorter events, 9.2 us)
Async XLA Ops:
  6.5 168.0 %copy-start = (bf16[1,768,2048]{2,1,0:T(8,128)(2,1)S(1)}, bf16[1,768,2048]{2,1,0:T(8,128)(2,1)}, u32[]{:S(2)}) copy-start(bf16[1,768,2048]{2,1,0:T(8,128)(2,1)} %param.33) | copy-start | bytes 9437188
  9.2 4.9 %copy-start.11 = (f32[512]{0:T(512)S(1)}, f32[512]{0:T(512)}, u32[]{:S(2)}) copy-start(f32[512]{0:T(512)} %param.24) | copy-start | bytes 6148
  12.1 0.8 copy-start.4
  16.8 37.4 %all-to-all-start = ((bf16[8,256,576]{1,2,0:T(8,128)(2,1)}), bf16[8,256,576]{1,2,0:T(8,128)(2,1)}, u32[]{:S(2)}, u32[]{:S(2)}) async-start(bf16[8,256,576]{1,2,0:T(8,128)(2,1)} %stack.2), calls=%async_computation | async-start | bytes 4718592 | tf_op jit(solution)/shard_map/all_to_all | solution.py:107
  25.2 2.7 %copy-start.12 = (s32[2,32,6]{1,0,2:T(2,128)S(1)}, s32[2,32,6]{1,0,2:T(2,128)}, u32[]{:S(2)}) copy-start(s32[2,32,6]{1,0,2:T(2,128)} %param.19) | copy-start | bytes 4612
  25.2 4.5 %copy-start.15 = (f32[2048]{0:T(1024)S(1)}, f32[2048]{0:T(1024)}, u32[]{:S(2)}) copy-start(f32[2048]{0:T(1024)} %param.21) | copy-start | bytes 24580
  25.2 105.7 %all-reduce.3.cloned.1.call-start = ((), (), s32[]{:S(2)}) async-start(), calls=%async_computation.4 | async-start | bytes 2097152 | tf_op jit(solution)/shard_map/psum | solution.py:153
  28.9 5.5 %copy-start.10 = (s32[64,3]{0,1:T(4,128)}, s32[64,3]{0,1:T(4,128)S(1)}, u32[]{:S(2)}) copy-start(s32[64,3]{0,1:T(4,128)S(1)} %reduce-window.9) | copy-start | bytes 2308
  32.1 0.8 copy-start.7
  54.3 2.0 copy-start.14
  56.3 1.4 copy-start.8
  57.7 1.3 copy-start.6
  59.0 1.0 copy-start.5
  60.0 1.9 copy-start.3
  67.4 2.8 %slice-start = ((s32[64,3]{0,1:T(4,128)}), s32[64,2]{0,1:T(2,128)S(1)}, s32[]{:S(2)}) async-start(s32[64,3]{0,1:T(4,128)} %copy-done.10), calls=%async_computation.6 | async-start | bytes 2048 | tf_op jit(solution)/shard_map/slice.1
  70.1 63.8 %copy-start.9 = (f32[2048]{0:T(1024)S(1)}, f32[2048]{0:T(1024)}, u32[]{:S(2)}) copy-start(f32[2048]{0:T(1024)} %param.27) | copy-start | bytes 24580
  132.9 1.0 copy-start.2
  134.2 1.0 copy-start.1
  138.9 29.4 %all-to-all-start.1 = ((bf16[64,4,2048]{2,1,0:T(4,128)(2,1)}), bf16[64,4,2048]{2,1,0:T(4,128)(2,1)}, u32[]{:S(2)}, u32[]{:S(2)}) async-start(bf16[64,4,2048]{2,1,0:T(4,128)(2,1)} %reshape.257), calls=%async_computation.2 | async-start | bytes 2097152 | tf_op jit(solution)/shard_map/all_to_all | solution.py:184
  149.8 58.5 %reduce-scatter.2.cloned.1.call-start = ((), (), s32[]{:S(2)}) async-start(), calls=%async_computation.5 | async-start | bytes 1179648 | tf_op jit(solution)/shard_map/reduce_scatter | solution.py:163
  180.1 7.7 %copy-start.13 = (f32[2,32,6]{1,0,2:T(2,128)S(1)}, f32[2,32,6]{1,0,2:T(2,128)}, u32[]{:S(2)}) copy-start(f32[2,32,6]{1,0,2:T(2,128)} %param.20) | copy-start | bytes 4612
  182.4 23.8 %all-to-all-start.2 = ((bf16[64,4,2048]{2,1,0:T(4,128)(2,1)}), bf16[64,4,2048]{2,1,0:T(4,128)(2,1)}, u32[]{:S(2)}, u32[]{:S(2)}) async-start(bf16[64,4,2048]{2,1,0:T(4,128)(2,1)} %reshape_transpose_reshape.4), calls=%async_computation.3 | async-start | bytes 2097152 | tf_op jit(solution)/shard_map/all_to_all | solution.py:202
Sparse Core Ops, SparseCore 0:
  70.3 60.5 all-reduce.2
  156.2 30.7 reduce-scatter.1
